TPU v7x, 256 devices: a whole 4x4x8 slice. The times are simulated.
256 devices in a mesh: tm: 16 (over y, x), space: 16 (over z, core).
Axes of the slice: x: 4, y: 4, z: 8, core: 2. Of those that a mesh axis runs over, the one named last changes fastest.
Arguments:
- query_heads: bfloat16 [32, 64, 64, 2240], P('tm', 'space'), may hold values from -10.5 to 10.5
- key_heads: bfloat16 [32, 64, 64, 2240], P('tm', 'space'), may hold values from -10.5 to 10.5
- value_heads: bfloat16 [32, 64, 64, 2240], P('tm', 'space'), may hold values from -12 to 12
- head_gain: float32 [2240], replicated, may hold values from 0.1 to 1.9
- spatial_kernel: float32 [9, 2240], replicated, may hold values from -2 to 2
- temporal_kernel: float32 [3, 2240], replicated, may hold values from -3.5 to 3.5
- out_weight: bfloat16 [2240, 2240], P('space', 'tm'), may hold values from -0.125 to 0.125
Outputs:
- mixed_out: bfloat16 [32, 64, 64, 2240], P('tm', 'space')
All inputs are finite; a program needn't handle non-finite values.
Results may differ from a plain program's by a relative error of at most 0.0057.
Values may be sent and summed in bfloat16 or wider, within the bound.
No kernel may reach another device: no remote copies, remote signals or barrier semaphores. Data moves between devices by JAX's collectives and lax.ppermute only.
A program may use at most 128 MiB of HBM per device.

v0:
```python
import jax
import jax.numpy as jnp
from jax import lax
from jax.sharding import PartitionSpec as P

HEADS = 20
HEAD_DIM = 112
epsilon = 1e-06


def entering(part, axis, combine, identity):
    place = lax.axis_index(axis)
    gathered = lax.all_gather(part, axis)
    state = jnp.zeros_like(part) + jnp.asarray(identity, part.dtype)

    def one(hop, state):
        return combine(state, lax.dynamic_index_in_dim(gathered, hop, 0, False))

    return lax.fori_loop(0, place, one, state)


def extended(block, sides, width):
    for axis, dim in sides:
        count = lax.axis_size(axis)
        forward = [(i, i + 1) for i in range(count - 1)]
        backward = [(target, source) for source, target in forward]
        low = lax.ppermute(
            lax.slice_in_dim(block, block.shape[dim] - width, None, axis=dim), axis, forward
        )
        high = lax.ppermute(lax.slice_in_dim(block, 0, width, axis=dim), axis, backward)
        block = jnp.concatenate([low, block, high], axis=dim)
    return block


def from_behind(block, axis, distance):
    devices = range(lax.axis_size(axis))
    route = [(i - distance, i) for i in devices if i - distance in devices]
    return lax.ppermute(block, axis, route)


def add_states(earlier, latter):
    return earlier + latter


def spatial_conv(padded, spatial_kernel):
    frame_count = padded.shape[0]
    row_count = padded.shape[1] - 2
    col_count = padded.shape[2]
    widened = jnp.pad(padded, ((0, 0), (0, 0), (1, 1), (0, 0)))
    summed = jnp.zeros((frame_count, row_count, col_count, padded.shape[3]), jnp.float32)
    for row_step in range(3):
        for col_step in range(3):
            summed = summed + spatial_kernel[3 * row_step + col_step] * widened[
                :, row_step : row_step + row_count, col_step : col_step + col_count
            ].astype(jnp.float32)
    return summed.astype(jnp.bfloat16)


def per_device(
    query_heads, key_heads, value_heads, head_gain, spatial_kernel, temporal_kernel, out_weight
):
    frame_count, row_count, col_count, model_width = query_heads.shape
    token_count = frame_count * row_count * col_count
    queries = query_heads.reshape(token_count, HEADS, HEAD_DIM)
    key_rows = key_heads.reshape(token_count, HEADS, HEAD_DIM)
    value_rows = value_heads.reshape(token_count, HEADS, HEAD_DIM)
    local_state = jnp.einsum(
        "thd,the->hde", jnp.maximum(key_rows, 0), value_rows, preferred_element_type=jnp.float32
    )
    summed = lax.psum(local_state, "space")
    earlier = entering(summed, "tm", add_states, jnp.zeros_like(summed))
    state_low = (earlier + summed).astype(jnp.bfloat16)
    attended = jnp.einsum(
        "thd,hde->the", jnp.maximum(queries, 0), state_low, preferred_element_type=jnp.float32
    )
    mean_square = jnp.mean(attended * attended, axis=-1, keepdims=True)
    normed = (attended * lax.rsqrt(mean_square + epsilon)).reshape(
        frame_count, row_count, col_count, model_width
    ) * head_gain
    padded = extended(value_heads, (("space", 1),), 1)
    spatial = spatial_conv(padded, spatial_kernel)
    earlier_frames = from_behind(spatial, "tm", 1)
    window = jnp.concatenate([earlier_frames, spatial], axis=0)
    temporal = jnp.zeros(normed.shape, jnp.float32)
    for back_step in range(3):
        temporal = temporal + temporal_kernel[back_step] * window[
            2 - back_step : 2 - back_step + frame_count
        ].astype(jnp.float32)
    mixed = (normed + temporal).astype(jnp.bfloat16).reshape(token_count, model_width)
    weight_band = lax.all_gather(out_weight, "tm", axis=1, tiled=True)
    projected = jnp.dot(
        mixed,
        lax.all_gather(weight_band, "space", axis=0, tiled=True),
        preferred_element_type=jnp.float32,
    )
    return projected.astype(jnp.bfloat16).reshape(frame_count, row_count, col_count, model_width)


def solution(mesh):
    placed = (
        P("tm", "space", None, None),
        P("tm", "space", None, None),
        P("tm", "space", None, None),
        P(),
        P(),
        P(),
        P("space", "tm"),
    )
    return jax.shard_map(
        per_device,
        mesh=mesh,
        in_specs=placed,
        out_specs=P("tm", "space", None, None),
        check_vma=False,
    )
```

profile of v0, /device:TPU:30, one launch (start us, length us, event | category | flops | bytes accessed | tf_op | source)
XLA Modules:
  0.0 405.4 jit_solution(10233113582889997337)
XLA Ops:
  6.5 0.0 all-reduce.3.cloned.1.call-start
  6.5 3.4 broadcast_maximum_fusion.1
  9.9 6.5 %max.13 = bf16[512,20,112]{2,1,0:T(8,128)(2,1)} reshape(bf16[2,4,64,2240]{3,2,1,0:T(8,128)(2,1)} %broadcast_maximum_fusion.1) | data formatting | bytes 4587520 | tf_op jit(solution)/shard_map/max | solution.py:68
  16.5 0.0 copy-done
  16.5 4.3 %reshape.39 = bf16[512,20,112]{2,1,0:T(8,128)(2,1)} reshape(bf16[2,4,64,2240]{3,2,1,0:T(8,128)(2,1)S(1)} %copy-done) | data formatting | bytes 4587520 | tf_op jit(solution)/shard_map/reshape | solution.py:66
  20.7 5.1 %fusion.9 = f32[20,112,112]{2,1,0:T(8,128)} fusion(bf16[512,20,112]{2,1,0:T(8,128)(2,1)} %reshape.39, bf16[512,20,112]{2,1,0:T(8,128)(2,1)} %max.13), kind=kOutput, calls=%fused_computation.17 | convolution fusion | flops 256901120 | bytes 5591040 | tf_op jit(solution)/shard_map/thd,the->hde/dot_general | solution.py:67
  25.8 0.0 all-reduce.3.cloned.1.call-update
  25.8 0.0 all-gather.8.cloned.1.call-start
  25.9 0.0 copy-done.3
  25.9 0.7 copy.26
  26.6 22.9 %all-gather.1 = bf16[16,140,140]{2,1,0:T(8,128)(2,1)S(1)} all-gather(bf16[1,140,140]{2,1,0:T(8,128)(2,1)} %bitcast.29), channel_id=1, replica_groups=mesh['tm'=16,'space'=16] {'tm'}, dimensions={0}, use_global_device_ids=true | all-gather | bytes 666400 | tf_op jit(solution)/shard_map/all_gather | solution.py:90
  49.5 1.2 reshape.48
  50.7 2.3 copy.30
  53.0 0.0 all-gather.8.cloned.1.call-update
  53.0 0.0 all-gather.6.cloned.1.call-start
  53.1 87.8 %all-reduce.3.cloned.1.call-done = f32[20,112,112]{2,1,0:T(8,128)} async-done(((f32[20,112,112]{2,1,0:T(8,128)}), f32[20,112,112]{2,1,0:T(8,128)}) %all-reduce.3.cloned.1.call-update) | async-done | bytes 1003536 | tf_op jit(solution)/shard_map/psum | solution.py:70
  140.9 0.0 all-gather.6.cloned.1.call-update
  140.9 0.0 copy-start.2
  140.9 0.1 fusion.12
  141.0 2.2 collective-permute-start
  143.3 1.3 collective-permute-start.1
  144.6 0.0 copy-done.4
  144.6 0.2 slice_reduce_fusion.10
  144.8 0.0 copy-done.2
  144.8 1.6 broadcast_maximum_fusion
  146.4 0.0 collective-permute-done
  146.4 0.7 collective-permute-done.1
  147.2 1.3 fusion.6
  148.4 0.0 copy-start.5
  148.5 5.9 %add_convert_fusion.1 = bf16[2,4,64,2240]{3,2,1,0:T(8,128)(2,1)} fusion(bf16[2,4,64,2240]{3,2,1,0:T(8,128)(2,1)S(1)} %copy-done, bf16[2,6,66,2240]{3,2,1,0:T(8,128)(2,1)S(1)} %fusion.6, bf16[2,1,64,2240]{3,2,1,0:T(8,128)(2,1)S(1)} %collective-permute-done.1, bf16[2,1,64,2240]{3,2,1,0:T(8,128)(2,1)S(1)} %collective-permute-done, ...), kind=kLoop, calls=%fused_computation.5 | loop fusion | flops 33259520 | bytes 19577600 | tf_op jit(solution)/shard_map/convert_element_type | solution.py:56
  154.3 1.3 collective-permute-start.2
  155.6 0.0 copy-done.5
  155.6 0.1 slice_reduce_fusion.11
  155.7 6.6 %max.15 = bf16[512,20,112]{2,1,0:T(8,128)(2,1)} reshape(bf16[2,4,64,2240]{3,2,1,0:T(8,128)(2,1)} %broadcast_maximum_fusion) | data formatting | bytes 4587520 | tf_op jit(solution)/shard_map/max | solution.py:74
  162.3 47.6 %all-gather.8.cloned.1.call-done = bf16[16,140,2240]{2,1,0:T(8,128)(2,1)} async-done(((bf16[1,140,2240]{2,1,0:T(8,128)(2,1)}), bf16[16,140,2240]{2,1,0:T(8,128)(2,1)}) %all-gather.8.cloned.1.call-update) | async-done | bytes 10035216 | tf_op jit(solution)/shard_map/all_gather | solution.py:93
  209.9 11.9 %reshape.47 = bf16[2240,2240]{1,0:T(8,128)(2,1)} reshape(bf16[16,140,2240]{2,1,0:T(8,128)(2,1)} %all-gather.8.cloned.1.call-done) | data formatting | bytes 20070400
  221.8 111.6 %all-gather.6.cloned.1.call-done = f32[320,112,112]{2,1,0:T(8,128)} async-done(((f32[20,112,112]{2,1,0:T(8,128)}), f32[320,112,112]{2,1,0:T(8,128)}) %all-gather.6.cloned.1.call-update) | async-done | bytes 16056336 | tf_op jit(solution)/shard_map/all_gather | solution.py:13
  333.3 0.1 broadcast_in_dim.2
  333.4 0.0 copy-start.1
  333.4 23.2 %while.10 = (s32[]{:T(128)}, f32[20,112,112]{2,1,0:T(8,128)S(1)}, s32[]{:T(128)}, f32[16,20,112,112]{3,2,1,0:T(8,128)}, s32[]{:T(128)}, /*index=5*/s32[]{:T(128)}, s32[]{:T(128)}) while((s32[]{:T(128)}, f32[20,112,112]{2,1,0:T(8,128)S(1)}, s32[]{:T(128)}, f32[16,20,112,112]{3,2,1,0:T(8,128)}, s32[]{:T(128)}, /*index=5*/s32[]{:T(128)}, ...), condition=%wide.region_2.3_spmd, body=%wide.region_1.2_spmd.sunk | while | flops 250885 | bytes 3010675 | solution.py:19
  333.4 1.6 bitcast_add_fusion.2
  335.0 1.5 bitcast_add_fusion.2
  336.6 1.5 bitcast_add_fusion.2
  338.1 1.5 bitcast_add_fusion.2
  339.6 1.5 bitcast_add_fusion.2
  341.2 1.5 bitcast_add_fusion.2
  342.7 1.5 bitcast_add_fusion.2
  344.2 1.5 bitcast_add_fusion.2
  345.7 1.5 bitcast_add_fusion.2
  347.3 1.5 bitcast_add_fusion.2
  348.8 1.5 bitcast_add_fusion.2
  350.3 1.5 bitcast_add_fusion.2
  351.8 1.5 bitcast_add_fusion.2
  353.4 1.5 bitcast_add_fusion.2
  354.9 1.5 bitcast_add_fusion.2
  356.6 0.0 copy-done.1
  356.6 2.9 fusion.4
  359.6 2.8 bitcast_multiply_fusion
  362.4 6.2 %copy.25 = f32[512,20,112]{2,1,0:T(8,128)} copy(f32[512,20,112]{0,2,1:T(8,128)} %bitcast_multiply_fusion) | data formatting | bytes 9175040 | tf_op jit(solution)/shard_map/mul | solution.py:77
  368.6 7.3 %reshape.40 = f32[2,4,64,2240]{3,2,1,0:T(8,128)} reshape(f32[512,20,112]{2,1,0:T(8,128)} %copy.25) | data formatting | bytes 9175040 | tf_op jit(solution)/shard_map/reshape | solution.py:77
  375.9 0.0 collective-permute-done.2
  375.9 5.4 %add_convert_fusion = bf16[2,4,64,2240]{3,2,1,0:T(8,128)(2,1)S(1)} fusion(bf16[2,4,64,2240]{3,2,1,0:T(8,128)(2,1)} %collective-permute-done.2, bf16[2,4,64,2240]{3,2,1,0:T(8,128)(2,1)} %add_convert_fusion.1, f32[2,4,64,2240]{3,2,1,0:T(8,128)} %reshape.40, f32[2240]{0:T(1024)S(1)} %get-tuple-element.39, f32[2240]{0:T(1024)S(1)} %get-tuple-element.40, ...), kind=kLoop, calls=%fused_computation.4 | loop fusion | flops 13762560 | bytes 11504640 | tf_op jit(solution)/shard_map/convert_element_type | solution.py:89
  381.3 13.4 %convolution_convert_fusion = bf16[512,2240]{0,1:T(8,128)(2,1)} fusion(bf16[512,2240]{1,0:T(8,128)(2,1)S(1)} %bitcast.27, bf16[2240,2240]{1,0:T(8,128)(2,1)} %reshape.47), kind=kOutput, calls=%fused_computation.12 | convolution fusion | flops 5139169280 | bytes 14622720 | tf_op jit(solution)/shard_map/dot_general | solution.py:91
  394.7 4.2 %copy.28 = bf16[512,2240]{1,0:T(8,128)(2,1)} copy(bf16[512,2240]{0,1:T(8,128)(2,1)} %convolution_convert_fusion) | data formatting | bytes 4587520 | tf_op jit(solution)/shard_map/convert_element_type | solution.py:96
  (6 shorter events, 0.0 us)
Async XLA Ops:
  6.5 9.9 %copy-start = (bf16[2,4,64,2240]{3,2,1,0:T(8,128)(2,1)S(1)}, bf16[2,4,64,2240]{3,2,1,0:T(8,128)(2,1)}, u32[]{:S(2)}) copy-start(bf16[2,4,64,2240]{3,2,1,0:T(8,128)(2,1)} %param.11) | copy-start | bytes 6881284
  6.5 134.3 %all-reduce.3.cloned.1.call-start = ((), (), s32[]{:S(2)}) async-start(), calls=%async_computation | async-start | bytes 2293760 | tf_op jit(solution)/shard_map/psum | solution.py:70
  20.7 5.1 %copy-start.3 = (bf16[140,140]{1,0:T(8,128)(2,1)S(1)}, bf16[140,140]{1,0:T(8,128)(2,1)}, u32[]{:S(2)}) copy-start(bf16[140,140]{1,0:T(8,128)(2,1)} %param.15) | copy-start | bytes 117604
  25.8 184.0 %all-gather.8.cloned.1.call-start = ((), (), s32[]{:S(2)}) async-start(), calls=%async_computation.2 | async-start | bytes 11280384 | tf_op jit(solution)/shard_map/all_gather | solution.py:93
  50.7 93.8 %copy-start.4 = (f32[9,2240]{1,0:T(8,128)S(1)}, f32[9,2240]{1,0:T(8,128)}, u32[]{:S(2)}) copy-start(f32[9,2240]{1,0:T(8,128)} %param.13) | copy-start | bytes 241924
  53.0 280.3 %all-gather.6.cloned.1.call-start = ((), (), s32[]{:S(2)}) async-start(), calls=%async_computation.1 | async-start | bytes 19496960 | tf_op jit(solution)/shard_map/all_gather | solution.py:13
  140.9 3.9 copy-start.2
  141.0 5.4 %collective-permute-start = (bf16[2,1,64,2240]{3,2,1,0:T(8,128)(2,1)S(1)}, bf16[2,1,64,2240]{3,2,1,0:T(8,128)(2,1)S(1)}, u32[]{:S(2)}, u32[]{:S(2)}) collective-permute-start(bf16[2,1,64,2240]{3,2,1,0:T(8,128)(2,1)S(1)} %get-tuple-element.49), channel_id=1, source_target_pairs={{0,1},{1,2},{2,3},{3,4},{4,5},{5,6},{6,7},{7,8},{8,9},{9,10},{10,1... | collective-permute-start | bytes 1720328 | tf_op jit(solution)/shard_map/ppermute | solution.py:27
  143.3 3.9 collective-permute-start.1
  148.4 7.2 %copy-start.5 = (f32[3,2240]{1,0:T(4,128)S(1)}, f32[3,2240]{1,0:T(4,128)}, u32[]{:S(2)}) copy-start(f32[3,2240]{1,0:T(4,128)} %param.14) | copy-start | bytes 80644
  154.3 221.6 %collective-permute-start.2 = (bf16[2,4,64,2240]{3,2,1,0:T(8,128)(2,1)}, bf16[2,4,64,2240]{3,2,1,0:T(8,128)(2,1)}, u32[]{:S(2)}, u32[]{:S(2)}) collective-permute-start(bf16[2,4,64,2240]{3,2,1,0:T(8,128)(2,1)} %add_convert_fusion.1), channel_id=1, source_target_pairs={{0,16},{16,32},{32,48},{48,64},{64,80},{80,96},{96,112},{112,128},... | collective-permute-start | bytes 6881288 | tf_op jit(solution)/shard_map/ppermute | solution.py:38
  333.4 23.2 %copy-start.1 = (f32[20,112,112]{2,1,0:T(8,128)S(1)}, f32[20,112,112]{2,1,0:T(8,128)}, u32[]{:S(2)}) copy-start(f32[20,112,112]{2,1,0:T(8,128)} %all-reduce.3.cloned.1.call-done) | copy-start | bytes 3010564
  368.6 7.3 %copy-start.6 = (f32[2240]{0:T(1024)S(1)}, f32[2240]{0:T(1024)}, u32[]{:S(2)}) copy-start(f32[2240]{0:T(1024)} %param.12) | copy-start | bytes 26884
Sparse Core Ops, SparseCore 0:
  25.9 114.9 all-reduce.2
  142.7 67.0 all-gather.7
  212.3 120.9 all-gather.5
where the time goes:
time: 407 us; the launch traced here: 405 us
  waiting for transfers between devices  248 us (61%)
  local copies, waits for them, and re-layouts  51.7 us (13%)
  other arithmetic  42.9 us (11%)
  blocking collectives  22.9 us (6%)
  matrix products  21.4 us (5%)
  between operations  13.3 us (3%)
  starting transfers between devices  4.89 us (1%)
    all_gather x1, waiting for transfers between devices, entering(): gathered = lax.all_gather(part, axis)  112 us
    psum x1, waiting for transfers between devices, per_device(): summed = lax.psum(local_state, 'space')  87.8 us
    all_gather x1, waiting for transfers between devices, per_device(): lax.all_gather(weight_band, 'space', axis=0, tiled=True)  47.6 us
    all_gather x1, blocking collectives, per_device(): weight_band = lax.all_gather(out_weight, 'tm', axis=1, tiled=True)  22.9 us
    add x15, other arithmetic, add_states(): return earlier + latter  22.6 us
    unnamed x18, local copies, waits for them, and re-layouts  16.2 us
    dot_general x1, matrix products, per_device(): jnp.dot(mixed, lax.all_gather(weight_band, 'space', axis=0, tiled=True),...  13.4 us
  transfers between devices with their start and end apart: 6, of which 4 were waited for; matrix products, arithmetic and copies ran while one was open for 18% of the time, Pallas kernels for 0%

commit v1 on v0

--- a/solution.py
+++ b/solution.py
@@ -90,7 +90,9 @@
     weight_band = lax.all_gather(out_weight, "tm", axis=1, tiled=True)
     projected = jnp.dot(
         mixed,
-        lax.all_gather(weight_band, "space", axis=0, tiled=True),
+        jnp.concatenate(
+            lax.all_to_all(jnp.stack([weight_band] * lax.axis_size("space")), "space", 0, 0), axis=0
+        ),
         preferred_element_type=jnp.float32,
     )
     return projected.astype(jnp.bfloat16).reshape(frame_count, row_count, col_count, model_width)

time: 407 us -> 512 us (1.26)
  the two profiles are of different devices: /device:TPU:30 before, /device:TPU:29 now
where the time goes in v1:
time: 512 us; the launch traced here: 511 us
  waiting for transfers between devices  344 us (67%)
  local copies, waits for them, and re-layouts  54 us (11%)
  other arithmetic  41.4 us (8%)
  starting transfers between devices  21.2 us (4%)
  blocking collectives  19.4 us (4%)
  matrix products  16.5 us (3%)
  between operations  13.6 us (3%)
    ppermute x1, waiting for transfers between devices, extended(): lax.ppermute(lax.slice_in_dim(block, block.shape[dim] - width, None, axis...  227 us
    psum x1, waiting for transfers between devices, per_device(): summed = lax.psum(local_state, 'space')  115 us
    add x14, other arithmetic, add_states(): return earlier + latter  21.1 us
    all_gather x1, blocking collectives, per_device(): weight_band = lax.all_gather(out_weight, 'tm', axis=1, tiled=True)  19.4 us
    all_to_all x1, starting transfers between devices, per_device(): lax.all_to_all(jnp.stack([weight_band] * lax.axis_size('space')), 'space'...  12.8 us
    reshape x1, local copies, waits for them, and re-layouts, per_device(): jnp.concatenate(lax.all_to_all(jnp.stack([weight_band] * lax.axis_size('s...  11.9 us
  transfers between devices with their start and end apart: 6, of which 3 were waited for; matrix products, arithmetic and copies ran while one was open for 15% of the time, Pallas kernels for 0%

profile of v1, /device:TPU:29, one launch (start us, length us, event | category | flops | bytes accessed | tf_op | source)
XLA Modules:
  0.0 510.9 jit_solution(12124587281421820721)
XLA Ops:
  6.5 0.0 copy-start
  6.5 0.0 all-reduce.3.cloned.1.call-start
  6.5 3.4 broadcast_maximum_fusion.1
  9.9 6.5 %max.13 = bf16[512,20,112]{2,1,0:T(8,128)(2,1)} reshape(bf16[2,4,64,2240]{3,2,1,0:T(8,128)(2,1)} %broadcast_maximum_fusion.1) | data formatting | bytes 4587520 | tf_op jit(solution)/shard_map/max | solution.py:68
  16.5 0.0 copy-done
  16.5 4.3 reshape.44
  20.7 0.0 copy-start.3
  20.7 5.0 fusion.9
  25.8 0.0 all-reduce.3.cloned.1.call-update
  25.8 0.0 all-gather.4.cloned.1.call-start
  25.9 115.4 %all-reduce.3.cloned.1.call-done = f32[20,112,112]{2,1,0:T(8,128)} async-done(((f32[20,112,112]{2,1,0:T(8,128)}), f32[20,112,112]{2,1,0:T(8,128)}) %all-reduce.3.cloned.1.call-update) | async-done | bytes 1003536 | tf_op jit(solution)/shard_map/psum | solution.py:70
  141.2 0.0 all-gather.4.cloned.1.call-update
  141.3 0.0 copy-done.3
  141.3 0.7 copy.27
  142.0 19.4 %all-gather.1 = bf16[16,140,140]{2,1,0:T(8,128)(2,1)S(1)} all-gather(bf16[1,140,140]{2,1,0:T(8,128)(2,1)} %bitcast.27), channel_id=1, replica_groups=mesh['tm'=16,'space'=16] {'tm'}, dimensions={0}, use_global_device_ids=true | all-gather | bytes 666400 | tf_op jit(solution)/shard_map/all_gather | solution.py:90
  161.4 1.2 reshape.52
  162.6 1.6 copy.31
  164.3 4.6 stack.2
  168.9 12.8 %all-to-all-start = ((bf16[16,140,2240]{2,1,0:T(8,128)(2,1)}), bf16[16,140,2240]{2,1,0:T(8,128)(2,1)}, u32[]{:S(2)}, u32[]{:S(2)}) async-start(bf16[16,140,2240]{2,1,0:T(8,128)(2,1)} %stack.2), calls=%async_computation | async-start | bytes 21233664 | tf_op jit(solution)/shard_map/all_to_all | solution.py:94
  181.7 0.1 fusion.12
  181.8 3.7 collective-permute-start
  185.5 1.9 collective-permute-start.1
  187.4 0.0 copy-done.4
  187.4 0.2 slice_reduce_fusion.10
  187.6 0.0 copy-done.2
  187.7 1.6 broadcast_maximum_fusion
  189.3 227.2 %collective-permute-done = bf16[2,1,64,2240]{3,2,1,0:T(8,128)(2,1)S(1)} collective-permute-done((bf16[2,1,64,2240]{3,2,1,0:T(8,128)(2,1)S(1)}, bf16[2,1,64,2240]{3,2,1,0:T(8,128)(2,1)S(1)}, u32[]{:S(2)}, u32[]{:S(2)}) %collective-permute-start) | collective-permute-done | bytes 573472 | tf_op jit(solution)/shard_map/ppermute | solution.py:27
  416.5 1.7 collective-permute-done.1
  418.2 1.3 fusion.6
  419.5 0.0 copy-start.5
  419.5 5.9 %add_convert_fusion.1 = bf16[2,4,64,2240]{3,2,1,0:T(8,128)(2,1)} fusion(bf16[2,4,64,2240]{3,2,1,0:T(8,128)(2,1)S(1)} %copy-done, bf16[2,6,66,2240]{3,2,1,0:T(8,128)(2,1)S(1)} %fusion.6, bf16[2,1,64,2240]{3,2,1,0:T(8,128)(2,1)S(1)} %collective-permute-done.1, bf16[2,1,64,2240]{3,2,1,0:T(8,128)(2,1)S(1)} %collective-permute-done, ...), kind=kLoop, calls=%fused_computation.5 | loop fusion | flops 33259520 | bytes 19577600 | tf_op jit(solution)/shard_map/convert_element_type | solution.py:56
  425.4 2.8 collective-permute-start.2
  428.1 0.0 copy-done.5
  428.1 0.1 slice_reduce_fusion.11
  428.2 6.5 %max.15 = bf16[512,20,112]{2,1,0:T(8,128)(2,1)} reshape(bf16[2,4,64,2240]{3,2,1,0:T(8,128)(2,1)} %broadcast_maximum_fusion) | data formatting | bytes 4587520 | tf_op jit(solution)/shard_map/max | solution.py:74
  434.8 0.0 all-to-all-done
  434.8 11.9 %reshape.47 = bf16[2240,2240]{1,0:T(8,128)(2,1)} reshape(bf16[16,140,2240]{2,1,0:T(8,128)(2,1)} %all-to-all-done) | data formatting | bytes 20070400 | tf_op jit(solution)/shard_map/reshape | solution.py:93
  446.7 0.1 broadcast_in_dim.2
  446.7 0.0 copy-start.1
  446.7 21.7 %while.10 = (s32[]{:T(128)}, f32[20,112,112]{2,1,0:T(8,128)S(1)}, s32[]{:T(128)}, f32[16,20,112,112]{3,2,1,0:T(8,128)}, s32[]{:T(128)}, /*index=5*/s32[]{:T(128)}, s32[]{:T(128)}) while((s32[]{:T(128)}, f32[20,112,112]{2,1,0:T(8,128)S(1)}, s32[]{:T(128)}, f32[16,20,112,112]{3,2,1,0:T(8,128)}, s32[]{:T(128)}, /*index=5*/s32[]{:T(128)}, ...), condition=%wide.region_2.3_spmd, body=%wide.region_1.2_spmd.sunk | while | flops 250885 | bytes 3010675 | solution.py:19
  446.8 1.6 bitcast_add_fusion.2
  448.4 1.5 bitcast_add_fusion.2
  449.9 1.5 bitcast_add_fusion.2
  451.4 1.5 bitcast_add_fusion.2
  453.0 1.5 bitcast_add_fusion.2
  454.5 1.5 bitcast_add_fusion.2
  456.0 1.5 bitcast_add_fusion.2
  457.5 1.5 bitcast_add_fusion.2
  459.1 1.5 bitcast_add_fusion.2
  460.6 1.5 bitcast_add_fusion.2
  462.1 1.5 bitcast_add_fusion.2
  463.7 1.5 bitcast_add_fusion.2
  465.2 1.5 bitcast_add_fusion.2
  466.7 1.5 bitcast_add_fusion.2
  468.4 0.0 copy-done.1
  468.4 3.0 fusion.4
  471.4 2.8 bitcast_multiply_fusion
  474.2 6.2 %copy.26 = f32[512,20,112]{2,1,0:T(8,128)} copy(f32[512,20,112]{0,2,1:T(8,128)} %bitcast_multiply_fusion) | data formatting | bytes 9175040 | tf_op jit(solution)/shard_map/mul | solution.py:77
  480.4 7.3 %reshape.45 = f32[2,4,64,2240]{3,2,1,0:T(8,128)} reshape(f32[512,20,112]{2,1,0:T(8,128)} %copy.26) | data formatting | bytes 9175040 | tf_op jit(solution)/shard_map/reshape | solution.py:77
  487.7 0.0 collective-permute-done.2
  487.7 0.0 copy-done.6
  487.7 5.4 %add_convert_fusion = bf16[2,4,64,2240]{3,2,1,0:T(8,128)(2,1)S(1)} fusion(bf16[2,4,64,2240]{3,2,1,0:T(8,128)(2,1)} %collective-permute-done.2, bf16[2,4,64,2240]{3,2,1,0:T(8,128)(2,1)} %add_convert_fusion.1, f32[2,4,64,2240]{3,2,1,0:T(8,128)} %reshape.45, f32[2240]{0:T(1024)S(1)} %get-tuple-element.39, f32[2240]{0:T(1024)S(1)} %get-tuple-element.40, ...), kind=kLoop, calls=%fused_computation.4 | loop fusion | flops 13762560 | bytes 11504640 | tf_op jit(solution)/shard_map/convert_element_type | solution.py:89
  493.1 8.5 %convolution_convert_fusion = bf16[512,2240]{0,1:T(8,128)(2,1)S(1)} fusion(bf16[512,2240]{1,0:T(8,128)(2,1)S(1)} %bitcast.25, bf16[2240,2240]{1,0:T(8,128)(2,1)} %reshape.47), kind=kOutput, calls=%fused_computation.12 | convolution fusion | flops 5139169280 | bytes 14622720 | tf_op jit(solution)/shard_map/dot_general | solution.py:91
  501.5 2.5 copy.29
  (5 shorter events, 0.0 us)
Async XLA Ops:
  6.5 9.9 %copy-start = (bf16[2,4,64,2240]{3,2,1,0:T(8,128)(2,1)S(1)}, bf16[2,4,64,2240]{3,2,1,0:T(8,128)(2,1)}, u32[]{:S(2)}) copy-start(bf16[2,4,64,2240]{3,2,1,0:T(8,128)(2,1)} %param.11) | copy-start | bytes 6881284
  6.5 134.7 %all-reduce.3.cloned.1.call-start = ((), (), s32[]{:S(2)}) async-start(), calls=%async_computation.1 | async-start | bytes 2293760 | tf_op jit(solution)/shard_map/psum | solution.py:70
  20.7 120.5 %copy-start.3 = (bf16[140,140]{1,0:T(8,128)(2,1)S(1)}, bf16[140,140]{1,0:T(8,128)(2,1)}, u32[]{:S(2)}) copy-start(bf16[140,140]{1,0:T(8,128)(2,1)} %param.15) | copy-start | bytes 117604
  25.8 420.8 %all-gather.4.cloned.1.call-start = ((), (), s32[]{:S(2)}) async-start(), calls=%async_computation.2 | async-start | bytes 19496960 | tf_op jit(solution)/shard_map/all_gather | solution.py:13
  168.9 18.5 %copy-start.4 = (f32[9,2240]{1,0:T(8,128)S(1)}, f32[9,2240]{1,0:T(8,128)}, u32[]{:S(2)}) copy-start(f32[9,2240]{1,0:T(8,128)} %param.13) | copy-start | bytes 241924
  168.9 265.8 %all-to-all-start = ((bf16[16,140,2240]{2,1,0:T(8,128)(2,1)}), bf16[16,140,2240]{2,1,0:T(8,128)(2,1)}, u32[]{:S(2)}, u32[]{:S(2)}) async-start(bf16[16,140,2240]{2,1,0:T(8,128)(2,1)} %stack.2), calls=%async_computation | async-start | bytes 21233664 | tf_op jit(solution)/shard_map/all_to_all | solution.py:94
  181.7 5.9 %copy-start.2 = (bf16[2,4,64,2240]{3,2,1,0:T(8,128)(2,1)S(1)}, bf16[2,4,64,2240]{3,2,1,0:T(8,128)(2,1)}, u32[]{:S(2)}) copy-start(bf16[2,4,64,2240]{3,2,1,0:T(8,128)(2,1)} %param.9) | copy-start | bytes 6881284
  181.8 234.7 %collective-permute-start = (bf16[2,1,64,2240]{3,2,1,0:T(8,128)(2,1)S(1)}, bf16[2,1,64,2240]{3,2,1,0:T(8,128)(2,1)S(1)}, u32[]{:S(2)}, u32[]{:S(2)}) collective-permute-start(bf16[2,1,64,2240]{3,2,1,0:T(8,128)(2,1)S(1)} %get-tuple-element.49), channel_id=1, source_target_pairs={{0,1},{1,2},{2,3},{3,4},{4,5},{5,6},{6,7},{7,8},{8,9},{9,10},{10,1... | collective-permute-start | bytes 1720328 | tf_op jit(solution)/shard_map/ppermute | solution.py:27
  185.5 232.7 %collective-permute-start.1 = (bf16[2,1,64,2240]{3,2,1,0:T(8,128)(2,1)S(1)}, bf16[2,1,64,2240]{3,2,1,0:T(8,128)(2,1)S(1)}, u32[]{:S(2)}, u32[]{:S(2)}) collective-permute-start(bf16[2,1,64,2240]{3,2,1,0:T(8,128)(2,1)S(1)} %get-tuple-element.50), channel_id=1, source_target_pairs={{1,0},{2,1},{3,2},{4,3},{5,4},{6,5},{7,6},{8,7},{9,8},{10,9},{11,1... | collective-permute-start | bytes 1720328 | tf_op jit(solution)/shard_map/ppermute | solution.py:30
  419.5 8.6 %copy-start.5 = (f32[3,2240]{1,0:T(4,128)S(1)}, f32[3,2240]{1,0:T(4,128)}, u32[]{:S(2)}) copy-start(f32[3,2240]{1,0:T(4,128)} %param.14) | copy-start | bytes 80644
  425.4 62.3 %collective-permute-start.2 = (bf16[2,4,64,2240]{3,2,1,0:T(8,128)(2,1)}, bf16[2,4,64,2240]{3,2,1,0:T(8,128)(2,1)}, u32[]{:S(2)}, u32[]{:S(2)}) collective-permute-start(bf16[2,4,64,2240]{3,2,1,0:T(8,128)(2,1)} %add_convert_fusion.1), channel_id=1, source_target_pairs={{0,16},{16,32},{32,48},{48,64},{64,80},{80,96},{96,112},{112,128},... | collective-permute-start | bytes 6881288 | tf_op jit(solution)/shard_map/ppermute | solution.py:38
  446.7 21.7 %copy-start.1 = (f32[20,112,112]{2,1,0:T(8,128)S(1)}, f32[20,112,112]{2,1,0:T(8,128)}, u32[]{:S(2)}) copy-start(f32[20,112,112]{2,1,0:T(8,128)} %all-reduce.3.cloned.1.call-done) | copy-start | bytes 3010564
  480.4 7.3 %copy-start.6 = (f32[2240]{0:T(1024)S(1)}, f32[2240]{0:T(1024)}, u32[]{:S(2)}) copy-start(f32[2240]{0:T(1024)} %param.12) | copy-start | bytes 26884
Sparse Core Ops, SparseCore 0:
  25.9 115.2 all-reduce.2
  143.7 148.7 all-gather.3
